TPU v7x, 256 devices: a whole 4x4x8 slice. The times are simulated.
256 devices in a mesh: dom: 16 (over x, y), slab: 16 (over z, core).
Axes of the slice: x: 4, y: 4, z: 8, core: 2. Of those that a mesh axis runs over, the one named last changes fastest.
Arguments:
- images: bfloat16 [4096, 8192], P(('dom', 'slab')), may hold values from -64 to 64
- defocus: bfloat16 [4096], P(('dom', 'slab')), may hold values from 20 to 60
- inv_noise: float32 [4096], replicated, may hold values from 0.01 to 0.04
- slices: bfloat16 [128, 8192], P('slab'), may hold values from -5 to 5
- lists: int32 [4096, 32], P(('dom', 'slab')), may hold values from 0 to 127, as said below
- counts: int32 [4096], P(('dom', 'slab')), may hold values from 0 to 32, as said below
Outputs:
- peak_weight: float32 [4096], P(('dom', 'slab'))
- data_sum: float32 [128, 8192], P('slab', 'dom')
- weight_sum: float32 [128, 4096], P('slab', 'dom')
Inputs may be any that keep to these rules, and one draw needn't show every extreme that they name: `lists`: the 32 entries of a row are different orientations. `counts`: 0 marks a particle left out of this pass; a particle that takes part has 2 or more significant orientations.
All inputs are finite; a program needn't handle non-finite values.
Results may differ from a plain program's by a relative error of at most 0.009.
Values may be sent and summed in bfloat16 or wider, within the bound.
No kernel may reach another device: no remote copies, remote signals or barrier semaphores. Data moves between devices by JAX's collectives and lax.ppermute only.
A program may use at most 128 MiB of HBM per device.

v0:
```python
import math
import jax
import jax.numpy as jnp
from jax import lax
from jax.sharding import PartitionSpec as P

SIDE = 64
COEF = 4096
TRANS = 25
SENTINEL = -1e30
HIGHEST = lax.Precision.HIGHEST


def frequency_grid():
    position = jnp.arange(COEF, dtype=jnp.int32)
    freq_x = (position // SIDE - SIDE // 2).astype(jnp.float32)
    freq_y = (position % SIDE - SIDE // 2).astype(jnp.float32)
    return (freq_x, freq_y)


def shift_tables(freq_x, freq_y):
    edge = math.isqrt(TRANS)
    half = edge // 2
    offsets = jnp.arange(TRANS, dtype=jnp.int32)
    shift_x = (offsets // edge - half).astype(jnp.float32)
    shift_y = (offsets % edge - half).astype(jnp.float32)
    angle = (
        2.0
        * jnp.pi
        * (shift_x[:, None] * freq_x[None, :] + shift_y[:, None] * freq_y[None, :])
        / SIDE
    )
    return (jnp.cos(angle), jnp.sin(angle))


def rotate_rows(values, cosine, sine):
    real_part = values[:, None, :COEF]
    imag_part = values[:, None, COEF:]
    turned = jnp.concatenate(
        (real_part * cosine - imag_part * sine, real_part * sine + imag_part * cosine), axis=-1
    )
    return turned.reshape(values.shape[0] * TRANS, 2 * COEF)


def significance(lists, counts, offset, number):
    orient_ids = offset + jnp.arange(number, dtype=jnp.int32)
    slot_live = jnp.arange(lists.shape[1], dtype=jnp.int32)[None, :] < counts[:, None]
    hits = (lists[:, :, None] == orient_ids[None, None, :]) & slot_live[:, :, None]
    return jnp.any(hits, axis=1)


def expectation(
    images,
    defocus,
    lists,
    counts,
    inv_noise,
    slices,
    offset,
    tile,
    reduce_highest,
    reduce_normalizer,
):
    row_count = images.shape[0]
    orient_count = slices.shape[0]
    freq_x, freq_y = frequency_grid()
    cosine, sine = shift_tables(freq_x, freq_y)
    radius = (freq_x * freq_x + freq_y * freq_y) / (SIDE * SIDE)
    ordering = jnp.argsort((counts <= 0).astype(jnp.int32), stable=True)
    sorted_images = jnp.take(images, ordering, axis=0)
    sorted_defocus = jnp.take(defocus, ordering, axis=0)
    sorted_lists = jnp.take(lists, ordering, axis=0)
    sorted_counts = jnp.take(counts, ordering, axis=0)
    alive = sorted_counts > 0
    live_tiles = (jnp.sum(alive.astype(jnp.int32)) + tile - 1) // tile
    ctf = -jnp.sin(jnp.pi * sorted_defocus.astype(jnp.float32)[:, None] * radius[None, :] + 0.1)
    real_part = sorted_images[:, :COEF].astype(jnp.float32)
    imag_part = sorted_images[:, COEF:].astype(jnp.float32)
    weighted = jnp.concatenate(
        (inv_noise * ctf * real_part, inv_noise * ctf * imag_part), axis=-1
    ).astype(jnp.bfloat16)
    image_half = jnp.concatenate((ctf * real_part, ctf * imag_part), axis=-1).astype(jnp.bfloat16)
    quad_half = -0.5 * inv_noise * ctf * ctf
    quadratic = jnp.concatenate((quad_half, quad_half), axis=-1).astype(jnp.bfloat16)
    slices_wide = slices.astype(jnp.float32)
    squares = (slices_wide * slices_wide).astype(jnp.bfloat16)
    energy = lax.dot_general(
        quadratic, squares, (((1,), (1,)), ((), ())), preferred_element_type=jnp.float32
    )
    mask = significance(sorted_lists, sorted_counts, offset, orient_count)

    def score_step(tile_step, buffer):
        rows_weighted = weighted.astype(jnp.float32)
        linear = lax.dot_general(
            rotate_rows(rows_weighted, cosine, sine),
            slices_wide,
            (((1,), (1,)), ((), ())),
            precision=HIGHEST,
        )
        linear = linear.reshape(tile, TRANS, orient_count)
        score = jnp.where(mask[:, None, :], linear + energy[:, None, :], SENTINEL)
        return score

    start_buffer = jnp.full((row_count, TRANS, orient_count), SENTINEL, jnp.float32)
    buffer = lax.fori_loop(0, live_tiles, score_step, start_buffer)
    highest = reduce_highest(jnp.max(buffer, axis=(1, 2)))
    highest = jnp.where(alive, highest, 0.0)
    expo = jnp.where(buffer > 0.5 * SENTINEL, jnp.exp(buffer - highest[:, None, None]), 0.0)
    normalizer = reduce_normalizer(jnp.sum(expo, axis=(1, 2)))
    normalizer = jnp.where(alive, normalizer, 1.0)
    posterior_half = (expo / normalizer[:, None, None]).astype(jnp.bfloat16)
    peak_sorted = jnp.where(alive, 1.0 / normalizer, 0.0)
    peak_values = jnp.zeros((row_count,), jnp.float32).at[ordering].set(peak_sorted)

    def sum_step(tile_step, total):
        return total + lax.dot_general(
            posterior_half.astype(jnp.float32).reshape(tile * TRANS, orient_count),
            rotate_rows(image_half.astype(jnp.float32), cosine, sine),
            (((0,), (0,)), ((), ())),
            precision=HIGHEST,
        )

    data_sum = lax.fori_loop(
        0, live_tiles, sum_step, jnp.zeros((orient_count, 2 * COEF), jnp.float32)
    )
    per_orient = jnp.sum(posterior_half.astype(jnp.float32), axis=1)
    ctf_half = (ctf * ctf).astype(jnp.bfloat16).astype(jnp.float32)
    weight_sum = lax.dot_general(per_orient, ctf_half, (((0,), (0,)), ((), ())), precision=HIGHEST)
    return (peak_values, data_sum, weight_sum)


def keep_values(values):
    return values


def shards(images, defocus, inv_noise, slices, lists, counts):
    whole_slices = lax.all_gather(slices, "slab", axis=0, tiled=True)
    peak_weight, data_sum, weight_sum = expectation(
        images, defocus, lists, counts, inv_noise, whole_slices, 0, 16, keep_values, keep_values
    )
    data_sum, weight_sum = (
        lax.psum_scatter(data_sum, "slab", scatter_dimension=0, tiled=True),
        lax.psum_scatter(weight_sum, "slab", scatter_dimension=0, tiled=True),
    )
    data_sum, weight_sum = (
        lax.psum_scatter(data_sum, "dom", scatter_dimension=1, tiled=True),
        lax.psum_scatter(weight_sum, "dom", scatter_dimension=1, tiled=True),
    )
    return (peak_weight, data_sum, weight_sum)


def solution(mesh):
    placed = (
        P(("dom", "slab"), None),
        P(("dom", "slab")),
        P(),
        P("slab", None),
        P(("dom", "slab"), None),
        P(("dom", "slab")),
    )
    return jax.shard_map(
        shards,
        mesh=mesh,
        in_specs=placed,
        out_specs=(P(("dom", "slab")), P("slab", "dom"), P("slab", "dom")),
        check_vma=False,
    )
```

profile of v0, /device:TPU:2, one launch (start us, length us, event | category | flops | bytes accessed | tf_op | source)
XLA Modules:
  0.0 366.6 jit_solution(13582859348225433491)
XLA Ops:
  7.2 0.7 all-gather.2.cloned.1.call-update
  8.0 0.7 compare_convert_fusion
  8.6 1.2 sort.17
  9.9 1.3 gather_fusion
  11.2 1.3 gather_fusion.2
  14.0 1.3 gather_fusion.1
  15.3 0.7 broadcast_multiply_fusion
  16.0 0.7 gather_fusion.3
  17.1 1.8 fusion.25
  18.9 1.9 fusion.24
  20.9 7.0 %multiply_subtract_fusion.1 = (f32[16,25,4096]{2,1,0:T(8,128)}, f32[16,25,4096]{2,1,0:T(8,128)}) fusion(f32[25,4096]{1,0:T(8,128)S(1)} %get-tuple-element.288, f32[16,4096]{1,0:T(8,128)S(1)} %get-tuple-element.282, f32[25,4096]{1,0:T(8,128)S(1)} %get-tuple-element.287, f32[16,4096]{1,0:T(8,128)S(1)} %get-tuple-element.281), kind=kLoop, calls=%fused_computation.25 | loop fusion | flops 9830400 | bytes 14450688 | tf_op jit(solution)/shard_map/while/body/sub | solution.py:40
  27.9 24.3 %all-gather.2.cloned.1.call-done = bf16[128,8192]{1,0:T(8,128)(2,1)} async-done(((bf16[8,8192]{1,0:T(8,128)(2,1)}), bf16[128,8192]{1,0:T(8,128)(2,1)}) %all-gather.2.cloned.1.call-update) | async-done | bytes 2097168 | tf_op jit(solution)/shard_map/all_gather | solution.py:137
  52.2 2.2 fusion.21
  54.5 12.4 %fusion.17 = f32[16,25,128]{2,1,0:T(8,128)S(1)} fusion(f32[16,25,4096]{2,1,0:T(8,128)} %get-tuple-element.280, f32[16,25,4096]{2,1,0:T(8,128)} %get-tuple-element.279, bf16[128,8192]{1,0:T(8,128)(2,1)} %all-gather.2.cloned.1.call-done), kind=kOutput, calls=%fused_computation.20 | convolution fusion | flops 5036441600 | bytes 15409152 | tf_op jit(solution)/shard_map/while/body/dot_general | solution.py:94
  66.9 0.7 broadcast_in_dim.63
  67.6 0.7 while.25
  67.6 0.7 add_select_fusion.3
  68.3 1.2 reduce_max.9
  69.5 1.3 fusion.37
  70.8 1.1 convert_reduce_fusion
  71.9 3.0 fusion.38
  75.0 2.2 broadcast_in_dim.94
  77.2 29.6 %while.26 = (s32[]{:T(128)}, f32[128,8192]{0,1:T(8,128)}, s32[]{:T(128)}, bf16[16,8192]{1,0:T(8,128)(2,1)S(1)}, bf16[16,25,128]{2,1,0:T(8,128)(2,1)S(1)}, /*inde...) while((s32[]{:T(128)}, f32[128,8192]{0,1:T(8,128)}, ...), condition=%wide.region_9.10_spmd.clone.clone.clone, body=%wide.region_8.9_spmd.clone.clone.clone.sunk | while | flops 5047730176 | bytes 37949740 | solution.py:123
  77.3 1.9 fusion.73
  79.2 7.0 %multiply_subtract_fusion.3 = (f32[16,25,4096]{2,1,0:T(8,128)}, f32[16,25,4096]{2,1,0:T(8,128)}) fusion(f32[25,4096]{1,0:T(8,128)S(1)} %get-tuple-element.396, f32[16,4096]{1,0:T(8,128)S(1)} %get-tuple-element.397, f32[25,4096]{1,0:T(8,128)S(1)} %get-tuple-element.398, f32[16,4096]{1,0:T(8,128)S(1)} %get-tuple-element.399), kind=kLoop, calls=%fused_computation.15.clone.1 | loop fusion | flops 9830400 | bytes 14450688 | tf_op jit(solution)/shard_map/while/body/sub | solution.py:40
  86.2 20.6 %fusion.75 = f32[128,8192]{0,1:T(8,128)} fusion(f32[128,8192]{0,1:T(8,128)} %get-tuple-element.434, bf16[16,25,128]{2,1,0:T(8,128)(2,1)S(1)} %get-tuple-element.447, f32[16,25,4096]{2,1,0:T(8,128)} %get-tuple-element.400, f32[16,25,4096]{2,1,0:T(8,128)} %get-tuple-element.401), kind=kOutput, calls=%fused_computation.13.clone.1 | convolution fusion | flops 5037490176 | bytes 21598208 | tf_op jit(solution)/shard_map/while/body/dot_general | solution.py:116
  106.8 5.7 %copy.11 = f32[128,8192]{1,0:T(8,128)} copy(f32[128,8192]{0,1:T(8,128)} %get-tuple-element.146) | data formatting | bytes 8388608 | tf_op jit(solution)/shard_map/while | solution.py:123
  112.5 20.9 %reduce-scatter.9.cloned.1.call-done = f32[8,4096]{1,0:T(8,128)} async-done(((f32[128,4096]{1,0:T(8,128)}), f32[8,4096]{1,0:T(8,128)}) %reduce-scatter.9.cloned.1.call-update) | async-done | bytes 131088 | tf_op jit(solution)/shard_map/reduce_scatter | solution.py:143
  133.5 64.5 %reduce-scatter.5.cloned.1.call-done = f32[8,8192]{1,0:T(8,128)} async-done(((f32[128,8192]{1,0:T(8,128)}), f32[8,8192]{1,0:T(8,128)}) %reduce-scatter.5.cloned.1.call-update) | async-done | bytes 262160 | tf_op jit(solution)/shard_map/reduce_scatter | solution.py:142
  198.1 1.1 scatter_custom_fusion
  199.2 79.3 %reduce-scatter.11.cloned.1.call-done = f32[8,256]{1,0:T(8,128)} async-done(((f32[8,4096]{1,0:T(8,128)}), f32[8,256]{1,0:T(8,128)}) %reduce-scatter.11.cloned.1.call-update) | async-done | bytes 8208 | tf_op jit(solution)/shard_map/reduce_scatter | solution.py:147
  278.5 81.6 %reduce-scatter.7.cloned.1.call-done = f32[8,512]{1,0:T(8,128)} async-done(((f32[8,8192]{1,0:T(8,128)}), f32[8,512]{1,0:T(8,128)}) %reduce-scatter.7.cloned.1.call-update) | async-done | bytes 16400 | tf_op jit(solution)/shard_map/reduce_scatter | solution.py:146
  (28 shorter events, 1.6 us)
Async XLA Ops:
  7.2 8.9 %copy-start = (bf16[16,8192]{1,0:T(8,128)(2,1)S(1)}, bf16[16,8192]{1,0:T(8,128)(2,1)}, u32[]{:S(2)}) copy-start(bf16[16,8192]{1,0:T(8,128)(2,1)} %param.10) | copy-start | bytes 786436
  7.2 45.1 %all-gather.2.cloned.1.call-start = ((), (), s32[]{:S(2)}) async-start(), calls=%async_computation.4 | async-start | bytes 2228224 | tf_op jit(solution)/shard_map/all_gather | solution.py:137
  7.9 125.6 %reduce-scatter.9.cloned.1.call-start = ((), (), s32[]{:S(2)}) async-start(), calls=%async_computation.7 | async-start | bytes 2228224 | tf_op jit(solution)/shard_map/reduce_scatter | solution.py:143
  75.0 123.1 %reduce-scatter.5.cloned.1.call-start = ((), (), s32[]{:S(2)}) async-start(), calls=%async_computation.5 | async-start | bytes 4456448 | tf_op jit(solution)/shard_map/reduce_scatter | solution.py:142
  112.5 166.0 %reduce-scatter.11.cloned.1.call-start = ((), (), s32[]{:S(2)}) async-start(), calls=%async_computation.8 | async-start | bytes 139264 | tf_op jit(solution)/shard_map/reduce_scatter | solution.py:147
  133.5 226.6 %reduce-scatter.7.cloned.1.call-start = ((), (), s32[]{:S(2)}) async-start(), calls=%async_computation.6 | async-start | bytes 278528 | tf_op jit(solution)/shard_map/reduce_scatter | solution.py:146
Sparse Core Ops, SparseCore 0:
  9.8 42.3 all-gather.1
  75.1 58.3 reduce-scatter.8
  136.0 61.9 reduce-scatter.4
  201.9 76.4 reduce-scatter.10
  282.4 77.6 reduce-scatter.6
where the time goes:
time: 367 us
  waiting for transfers between devices  271 us (74%)
  matrix products  38.3 us (10%)
  other arithmetic  27.8 us (8%)
  between operations  14.6 us (4%)
  local copies, waits for them, and re-layouts  14.4 us (4%)
    reduce_scatter x1, waiting for transfers between devices, shards(): lax.psum_scatter(data_sum, 'dom', scatter_dimension=1, tiled=True)  81.6 us
    reduce_scatter x1, waiting for transfers between devices, shards(): lax.psum_scatter(weight_sum, 'dom', scatter_dimension=1, tiled=True)  79.3 us
    reduce_scatter x1, waiting for transfers between devices, shards(): lax.psum_scatter(data_sum, 'slab', scatter_dimension=0, tiled=True)  64.5 us
    all_gather x1, waiting for transfers between devices, shards(): whole_slices = lax.all_gather(slices, 'slab', axis=0, tiled=True)  24.3 us
    reduce_scatter x1, waiting for transfers between devices, shards(): lax.psum_scatter(weight_sum, 'slab', scatter_dimension=0, tiled=True)  20.9 us
    dot_general x1, matrix products, sum_step(): lax.dot_general(posterior_half.astype(jnp.float32).reshape(tile * TRANS,...  20.6 us
    sub x2, other arithmetic, rotate_rows(): real_part * cosine - imag_part * sine  14.1 us
    dot_general x1, matrix products, score_step(): lax.dot_general(rotate_rows(rows_weighted, cosine, sine), slices_wide, ((...  12.4 us
  transfers between devices with their start and end apart: 5, of which 5 were waited for; matrix products, arithmetic and copies ran while one was open for 16% of the time, Pallas kernels for 0%

commit v1 on v0

--- a/solution.py
+++ b/solution.py
@@ -134,7 +134,9 @@
 
 
 def shards(images, defocus, inv_noise, slices, lists, counts):
-    whole_slices = lax.all_gather(slices, "slab", axis=0, tiled=True)
+    whole_slices = jnp.concatenate(
+        lax.all_to_all(jnp.stack([slices] * lax.axis_size("slab")), "slab", 0, 0), axis=0
+    )
     peak_weight, data_sum, weight_sum = expectation(
         images, defocus, lists, counts, inv_noise, whole_slices, 0, 16, keep_values, keep_values
     )

time: 367 us -> 381 us (1.038)
  starting transfers between devices: 0.2 us -> 8.73 us
  waiting for transfers between devices: 271 us -> 277 us
    all_to_all x0 -> x1, waiting for transfers between devices: none -> 30 us  [shards(): lax.all_to_all(jnp.stack([slices] * lax.axis_size('slab')), 'slab', 0, 0)]
    all_gather x1 -> x0, waiting for transfers between devices: 24.3 us -> none  [shards(): whole_slices = lax.all_gather(slices, 'slab', axis=0, tiled=True)]
    all_to_all x0 -> x1, starting transfers between devices: none -> 8.57 us  [shards(): lax.all_to_all(jnp.stack([slices] * lax.axis_size('slab')), 'slab', 0, 0)]
  transfers between devices with their start and end apart: 5 -> 5, of which waited for: 5 -> 5; matrix products, arithmetic and copies ran while one was open for 16% -> 15% of each run, Pallas kernels for 0% -> 0%
where the time goes in v1:
time: 381 us
  waiting for transfers between devices  277 us (73%)
  matrix products  36.1 us (9%)
  other arithmetic  27 us (7%)
  local copies, waits for them, and re-layouts  16.9 us (4%)
  between operations  14.6 us (4%)
  starting transfers between devices  8.73 us (2%)
    reduce_scatter x1, waiting for transfers between devices, shards(): lax.psum_scatter(data_sum, 'dom', scatter_dimension=1, tiled=True)  81.7 us
    reduce_scatter x1, waiting for transfers between devices, shards(): lax.psum_scatter(weight_sum, 'dom', scatter_dimension=1, tiled=True)  79.3 us
    reduce_scatter x1, waiting for transfers between devices, shards(): lax.psum_scatter(data_sum, 'slab', scatter_dimension=0, tiled=True)  64.7 us
    all_to_all x1, waiting for transfers between devices, shards(): lax.all_to_all(jnp.stack([slices] * lax.axis_size('slab')), 'slab', 0, 0)  30 us
    reduce_scatter x1, waiting for transfers between devices, shards(): lax.psum_scatter(weight_sum, 'slab', scatter_dimension=0, tiled=True)  21.6 us
    dot_general x1, matrix products, sum_step(): lax.dot_general(posterior_half.astype(jnp.float32).reshape(tile * TRANS,...  20.5 us
    sub x2, other arithmetic, rotate_rows(): real_part * cosine - imag_part * sine  14 us
    dot_general x1, matrix products, score_step(): lax.dot_general(rotate_rows(rows_weighted, cosine, sine), slices_wide, ((...  11.9 us
  transfers between devices with their start and end apart: 5, of which 5 were waited for; matrix products, arithmetic and copies ran while one was open for 15% of the time, Pallas kernels for 0%

profile of v1, /device:TPU:2, one launch (start us, length us, event | category | flops | bytes accessed | tf_op | source)
XLA Modules:
  0.0 380.7 jit_solution(3970014028350118632)
XLA Ops:
  7.2 2.5 stack.2
  9.7 8.6 %all-to-all-start = ((bf16[16,8,8192]{2,1,0:T(8,128)(2,1)}), bf16[16,8,8192]{2,1,0:T(8,128)(2,1)S(1)}, u32[]{:S(2)}, u32[]{:S(2)}) async-start(bf16[16,8,8192]{2,1,0:T(8,128)(2,1)} %stack.2), calls=%async_computation | async-start | bytes 4194304 | tf_op jit(solution)/shard_map/all_to_all | solution.py:138
  18.3 0.7 compare_convert_fusion
  19.0 1.2 sort.17
  20.3 1.3 gather_fusion
  21.6 1.3 gather_fusion.2
  24.3 1.3 gather_fusion.1
  25.7 0.7 broadcast_multiply_fusion
  26.4 0.7 gather_fusion.3
  27.4 1.0 fusion.26
  28.6 1.9 fusion.25
  30.5 6.9 %multiply_subtract_fusion.1 = (f32[16,25,4096]{2,1,0:T(8,128)}, f32[16,25,4096]{2,1,0:T(8,128)}) fusion(f32[25,4096]{1,0:T(8,128)S(1)} %get-tuple-element.288, f32[16,4096]{1,0:T(8,128)S(1)} %get-tuple-element.282, f32[25,4096]{1,0:T(8,128)S(1)} %get-tuple-element.287, f32[16,4096]{1,0:T(8,128)S(1)} %get-tuple-element.281), kind=kLoop, calls=%fused_computation.25 | loop fusion | flops 9830400 | bytes 14450688 | tf_op jit(solution)/shard_map/while/body/sub | solution.py:40
  37.5 30.0 %all-to-all-done = bf16[16,8,8192]{2,1,0:T(8,128)(2,1)S(1)} async-done(((bf16[16,8,8192]{2,1,0:T(8,128)(2,1)}), bf16[16,8,8192]{2,1,0:T(8,128)(2,1)S(1)}, u32[]{:S(2)}, u32[]{:S(2)}) %all-to-all-start) | async-done | bytes 2097184 | tf_op jit(solution)/shard_map/all_to_all | solution.py:138
  68.1 11.9 %fusion.17 = f32[16,25,128]{2,1,0:T(8,128)S(1)} fusion(f32[16,25,4096]{2,1,0:T(8,128)} %get-tuple-element.280, f32[16,25,4096]{2,1,0:T(8,128)} %get-tuple-element.279, bf16[16,8,8192]{2,1,0:T(8,128)(2,1)S(1)} %all-to-all-done), kind=kOutput, calls=%fused_computation.20 | convolution fusion | flops 5036441600 | bytes 15409152 | tf_op jit(solution)/shard_map/while/body/dot_general | solution.py:94
  80.0 0.7 broadcast_in_dim.63
  80.8 0.7 while.25
  80.8 0.7 add_select_fusion.3
  81.5 1.2 reduce_max.9
  82.7 1.3 fusion.38
  83.9 1.1 convert_reduce_fusion
  85.1 3.0 fusion.39
  88.2 2.2 broadcast_in_dim.94
  90.4 29.6 %while.26 = (s32[]{:T(128)}, f32[128,8192]{0,1:T(8,128)}, s32[]{:T(128)}, bf16[16,8192]{1,0:T(8,128)(2,1)S(1)}, bf16[16,25,128]{2,1,0:T(8,128)(2,1)S(1)}, /*inde...) while((s32[]{:T(128)}, f32[128,8192]{0,1:T(8,128)}, ...), condition=%wide.region_9.10_spmd.clone.clone.clone, body=%wide.region_8.9_spmd.clone.clone.clone.sunk | while | flops 5047730176 | bytes 37949740 | solution.py:123
  90.4 1.9 fusion.74
  92.3 7.0 %multiply_subtract_fusion.3 = (f32[16,25,4096]{2,1,0:T(8,128)}, f32[16,25,4096]{2,1,0:T(8,128)}) fusion(f32[25,4096]{1,0:T(8,128)S(1)} %get-tuple-element.396, f32[16,4096]{1,0:T(8,128)S(1)} %get-tuple-element.397, f32[25,4096]{1,0:T(8,128)S(1)} %get-tuple-element.398, f32[16,4096]{1,0:T(8,128)S(1)} %get-tuple-element.399), kind=kLoop, calls=%fused_computation.15.clone.1 | loop fusion | flops 9830400 | bytes 14450688 | tf_op jit(solution)/shard_map/while/body/sub | solution.py:40
  99.4 20.5 %fusion.76 = f32[128,8192]{0,1:T(8,128)} fusion(f32[128,8192]{0,1:T(8,128)} %get-tuple-element.434, bf16[16,25,128]{2,1,0:T(8,128)(2,1)S(1)} %get-tuple-element.447, f32[16,25,4096]{2,1,0:T(8,128)} %get-tuple-element.400, f32[16,25,4096]{2,1,0:T(8,128)} %get-tuple-element.401), kind=kOutput, calls=%fused_computation.13.clone.1 | convolution fusion | flops 5037490176 | bytes 21598208 | tf_op jit(solution)/shard_map/while/body/dot_general | solution.py:116
  119.9 5.6 %copy.11 = f32[128,8192]{1,0:T(8,128)} copy(f32[128,8192]{0,1:T(8,128)} %get-tuple-element.146) | data formatting | bytes 8388608 | tf_op jit(solution)/shard_map/while | solution.py:123
  125.6 21.6 %reduce-scatter.9.cloned.1.call-done = f32[8,4096]{1,0:T(8,128)} async-done(((f32[128,4096]{1,0:T(8,128)}), f32[8,4096]{1,0:T(8,128)}) %reduce-scatter.9.cloned.1.call-update) | async-done | bytes 131088 | tf_op jit(solution)/shard_map/reduce_scatter | solution.py:145
  147.3 64.7 %reduce-scatter.5.cloned.1.call-done = f32[8,8192]{1,0:T(8,128)} async-done(((f32[128,8192]{1,0:T(8,128)}), f32[8,8192]{1,0:T(8,128)}) %reduce-scatter.5.cloned.1.call-update) | async-done | bytes 262160 | tf_op jit(solution)/shard_map/reduce_scatter | solution.py:144
  212.1 1.1 scatter_custom_fusion
  213.2 79.3 %reduce-scatter.11.cloned.1.call-done = f32[8,256]{1,0:T(8,128)} async-done(((f32[8,4096]{1,0:T(8,128)}), f32[8,256]{1,0:T(8,128)}) %reduce-scatter.11.cloned.1.call-update) | async-done | bytes 8208 | tf_op jit(solution)/shard_map/reduce_scatter | solution.py:149
  292.4 81.7 %reduce-scatter.7.cloned.1.call-done = f32[8,512]{1,0:T(8,128)} async-done(((f32[8,8192]{1,0:T(8,128)}), f32[8,512]{1,0:T(8,128)}) %reduce-scatter.7.cloned.1.call-update) | async-done | bytes 16400 | tf_op jit(solution)/shard_map/reduce_scatter | solution.py:148
  (30 shorter events, 2.2 us)
Async XLA Ops:
  7.2 19.2 %copy-start = (bf16[16,8192]{1,0:T(8,128)(2,1)S(1)}, bf16[16,8192]{1,0:T(8,128)(2,1)}, u32[]{:S(2)}) copy-start(bf16[16,8192]{1,0:T(8,128)(2,1)} %param.10) | copy-start | bytes 786436
  7.2 20.3 %copy-start.1 = (f32[4096]{0:T(1024)S(1)}, f32[4096]{0:T(1024)}, u32[]{:S(2)}) copy-start(f32[4096]{0:T(1024)} %param.12) | copy-start | bytes 49156
  9.7 57.8 %all-to-all-start = ((bf16[16,8,8192]{2,1,0:T(8,128)(2,1)}), bf16[16,8,8192]{2,1,0:T(8,128)(2,1)S(1)}, u32[]{:S(2)}, u32[]{:S(2)}) async-start(bf16[16,8,8192]{2,1,0:T(8,128)(2,1)} %stack.2), calls=%async_computation | async-start | bytes 4194304 | tf_op jit(solution)/shard_map/all_to_all | solution.py:138
  18.3 129.0 %reduce-scatter.9.cloned.1.call-start = ((), (), s32[]{:S(2)}) async-start(), calls=%async_computation.7 | async-start | bytes 2228224 | tf_op jit(solution)/shard_map/reduce_scatter | solution.py:145
  88.1 123.9 %reduce-scatter.5.cloned.1.call-start = ((), (), s32[]{:S(2)}) async-start(), calls=%async_computation.5 | async-start | bytes 4456448 | tf_op jit(solution)/shard_map/reduce_scatter | solution.py:144
  125.6 166.8 %reduce-scatter.11.cloned.1.call-start = ((), (), s32[]{:S(2)}) async-start(), calls=%async_computation.8 | async-start | bytes 139264 | tf_op jit(solution)/shard_map/reduce_scatter | solution.py:149
  147.3 226.9 %reduce-scatter.7.cloned.1.call-start = ((), (), s32[]{:S(2)}) async-start(), calls=%async_computation.6 | async-start | bytes 278528 | tf_op jit(solution)/shard_map/reduce_scatter | solution.py:148
Sparse Core Ops, SparseCore 0:
  88.2 58.9 reduce-scatter.8
  149.8 62.1 reduce-scatter.4
  216.1 76.3 reduce-scatter.10
  296.3 77.7 reduce-scatter.6
